TPU v7x, 128 devices: a whole 4x4x4 slice. The times are simulated.
128 devices in a mesh: tm: 64 (over x, y_hi, z, core), mp: 2 (over y_lo).
Axes of the slice: x: 4, y: 4 (y_hi: 2, y_lo: 2; y = y_hi * 2 + y_lo), z: 4, core: 2. Of those that a mesh axis runs over, the one named last changes fastest.
Arguments:
- frames: bfloat16 [32768, 1024], P('tm'), may hold values from -24 to 24
- cotangent: bfloat16 [32768, 1024], P('tm'), may hold values from -20 to 20
- weights: bfloat16 [1024, 4, 1024], P(None, None, 'mp'), may hold values from -4 to 4
- summary: bfloat16 [64, 1024], replicated, may hold values from -5 to 5
- owners: int32 [64], replicated, may hold values from 0 to 63, as said below
Outputs:
- grad_frames: bfloat16 [32768, 1024], P(('tm', 'mp'))
- grad_weights: float32 [1024, 4, 1024], P('tm', None, 'mp')
- grad_summary: float32 [64, 1024], replicated
Inputs may be any that keep to these rules, and one draw needn't show every extreme that they name: owners[g] is the index of the block of 512 frames that global token g summarizes.
All inputs are finite; a program needn't handle non-finite values.
Results may differ from a plain program's by a relative error of at most 0.04.
Values may be sent and summed in bfloat16 or wider, within the bound.
No kernel may reach another device: no remote copies, remote signals or barrier semaphores. Data moves between devices by JAX's collectives and lax.ppermute only.
A program may use at most 128 MiB of HBM per device.

v0:
```python
import numpy as np
import jax
import jax.numpy as jnp
from jax import lax
from jax.sharding import PartitionSpec as P

HEAD_DIM = 64
WINDOW = 512


EPSILON = 1e-05
PRECISE = lax.Precision.HIGHEST


def from_behind(shard, axis, by):
    devices = lax.axis_size(axis)
    pairs = [(i, i + by) for i in range(devices) if 0 <= i + by < devices]
    return lax.ppermute(shard, axis, pairs)


def tm_coords(i):
    return (i >> 4) & 3, (i >> 3) & 1, (i >> 1) & 3, i & 1


def tm_index(x, y_half, z, core):
    return ((x * 2 + y_half) * 4 + z) * 2 + core


def butterfly_plan():
    pairs, bits = [], np.zeros((64, 6), np.int32)
    flips = [("z", 1), ("x", 1), ("z", 2), ("x", 2), ("y", 1)]
    round_pairs = [[(i, i ^ 1) for i in range(64)]]
    for i in range(64):
        bits[i, 0] = i & 1
    for r, (axis, mask) in enumerate(flips):
        these = []
        for i in range(64):
            x, y_half, z, core = tm_coords(i)
            zl, xl = (z + core) % 4, (x + core) % 4
            label = {"z": zl, "x": xl, "y": y_half}[axis]
            bits[i, r + 1] = 1 if label & mask else 0
            if axis == "z":
                z = ((zl ^ mask) - core) % 4
            elif axis == "x":
                x = ((xl ^ mask) - core) % 4
            else:
                y_half ^= 1
            these.append((i, tm_index(x, y_half, z, core)))
        round_pairs.append(these)
    pairs = round_pairs
    return pairs, bits


def to_positions(a):
    rows = a.shape[0]
    r = a.reshape(rows, 4, 2, 4, 2, 16)
    first = r[:, :, :, :, 0, :]
    second = jnp.roll(jnp.roll(r[:, :, :, :, 1, :], 1, axis=1), 1, axis=3)
    g = jnp.stack([first, second], axis=1).reshape(rows, 2, 2, 2, 2, 2, 2, 16)
    g = g.transpose(0, 1, 6, 3, 5, 2, 4, 7)
    return g.reshape(rows, 1024)


def labels(i):
    x, y_half, z, core = tm_coords(i)
    return core, (z + core) % 4, (x + core) % 4, y_half


def from_labels(core, zl, xl, y_half):
    return tm_index((xl - core) % 4, y_half, (zl - core) % 4, core)


def radix_plan():
    steps = []
    keep = np.array([i & 1 for i in range(64)], np.int32)
    steps.append((2, keep, [([(i, i ^ 1) for i in range(64)], keep ^ 1)]))
    for mask, shift in ((1, 0), (2, 1)):
        keep = np.zeros(64, np.int32)
        for i in range(64):
            core, zl, xl, y_half = labels(i)
            keep[i] = ((zl & mask) >> shift) * 2 + ((xl & mask) >> shift)
        partners = []
        for d in (1, 2, 3):
            pairs = []
            for i in range(64):
                core, zl, xl, y_half = labels(i)
                zl ^= mask if d & 2 else 0
                xl ^= mask if d & 1 else 0
                pairs.append((i, from_labels(core, zl, xl, y_half)))
            partners.append((pairs, keep ^ d))
        steps.append((4, keep, partners))
    keep = np.array([labels(i)[3] for i in range(64)], np.int32)
    steps.append((2, keep, [([(i, i ^ 8) for i in range(64)], keep ^ 1)]))
    return steps


def glob_rounds():
    rounds = []
    for flip in ((1, 0), (0, 1), (2, 0), (0, 2)):
        pairs = []
        for i in range(64):
            core, zl, xl, y_half = labels(i)
            pairs.append((i, from_labels(core, zl ^ flip[0], xl ^ flip[1], y_half)))
        rounds.append(pairs)
    rounds.append([(i, i ^ 8) for i in range(64)])
    rounds.append([(i, i ^ 1) for i in range(64)])
    return rounds


def butterfly(parts, glob, shard_index):
    for ways, keep_table, partners in radix_plan():
        size = parts.shape[0] // ways
        kept = jnp.asarray(keep_table)[shard_index]
        total = lax.dynamic_slice_in_dim(parts, kept * size, size, 0)
        for pairs, send_table in partners:
            sent = jnp.asarray(send_table)[shard_index]
            total = total + lax.ppermute(
                lax.dynamic_slice_in_dim(parts, sent * size, size, 0), "tm", pairs
            )
        parts = total
    for pairs in glob_rounds():
        glob = glob + lax.ppermute(glob, "tm", pairs)
    glob = glob + lax.ppermute(glob, "mp", [(0, 1), (1, 0)])
    return parts, glob


def normalize(rows_in):
    inverse = lax.rsqrt(jnp.mean(rows_in * rows_in, axis=-1, keepdims=True) + EPSILON)
    return (rows_in * inverse, inverse)


def norm_back(gradient, unit_rows, inverse):
    return (gradient - unit_rows * jnp.mean(gradient * unit_rows, axis=-1, keepdims=True)) * inverse


def product(form, left, right):
    return jnp.einsum(form, left, right, preferred_element_type=jnp.float32)


def window_mask(row_count, lead, root):
    query_pos = lax.broadcasted_iota(jnp.int32, (row_count, row_count + lead), 0)
    key_pos = lax.broadcasted_iota(jnp.int32, (row_count, row_count + lead), 1)
    inside = (key_pos > query_pos) & (key_pos <= query_pos + lead)
    return inside & (root - lead + key_pos >= 0)


def block_pass(queries, keys_ext, values_ext, keys_glob, values_glob, grad_rows, allowed):
    scaling = HEAD_DIM ** (-0.5)
    near_scores = product("qhe,khe->hqk", queries, keys_ext) * scaling
    far_scores = product("qhe,khe->hqk", queries, keys_glob) * scaling
    near_scores = jnp.where(allowed[None, :, :], near_scores, -jnp.inf)
    row_top = jnp.maximum(
        jnp.max(near_scores, axis=-1, keepdims=True), jnp.max(far_scores, axis=-1, keepdims=True)
    )
    near_exp = jnp.exp(near_scores - row_top)
    far_exp = jnp.exp(far_scores - row_top)
    row_total = jnp.sum(near_exp, axis=-1, keepdims=True) + jnp.sum(far_exp, axis=-1, keepdims=True)
    near_prob = (near_exp / row_total).astype(jnp.bfloat16)
    far_prob = (far_exp / row_total).astype(jnp.bfloat16)
    attended = (
        product("hqk,khe->qhe", near_prob, values_ext)
        + product("hqk,khe->qhe", far_prob, values_glob)
    ).astype(jnp.bfloat16)
    near_dot = product("qhe,khe->hqk", grad_rows, values_ext)
    far_dot = product("qhe,khe->hqk", grad_rows, values_glob)
    near_p32 = near_prob.astype(jnp.float32)
    far_p32 = far_prob.astype(jnp.float32)
    row_delta = jnp.sum(near_p32 * near_dot, axis=-1, keepdims=True) + jnp.sum(
        far_p32 * far_dot, axis=-1, keepdims=True
    )
    near_grad = (near_p32 * (near_dot - row_delta) * scaling).astype(jnp.bfloat16)
    far_grad = (far_p32 * (far_dot - row_delta) * scaling).astype(jnp.bfloat16)
    query_grad = (
        product("hqk,khe->qhe", near_grad, keys_ext) + product("hqk,khe->qhe", far_grad, keys_glob)
    ).astype(jnp.bfloat16)
    key_grad = product("hqk,qhe->khe", near_grad, queries)
    value_grad = product("hqk,qhe->khe", near_prob, grad_rows)
    glob_key_grad = product("hqk,qhe->khe", far_grad, queries)
    glob_value_grad = product("hqk,qhe->khe", far_prob, grad_rows)
    return (attended, query_grad, key_grad, value_grad, glob_key_grad, glob_value_grad)


def shards(frames, cotangent, weights, summary, owners):
    rows_here = frames.shape[0]
    width = frames.shape[1]
    local_width = weights.shape[2]
    heads_here = local_width // HEAD_DIM
    glob_count = summary.shape[0]
    shard_index = lax.axis_index("tm")
    shard_total = lax.axis_size("tm")
    mp_index = lax.axis_index("mp")
    mp_total = lax.axis_size("mp")
    frames32 = frames.astype(jnp.float32)
    unit_rows, inverse = normalize(frames32)
    normed = unit_rows.astype(jnp.bfloat16)
    block_mean = jnp.mean(frames32, axis=0, keepdims=True)
    pool_unit, pool_inv = normalize(block_mean)
    pooled = pool_unit.astype(jnp.bfloat16)
    pooled_rows = jnp.concatenate([pooled, frames[1:8]], 0)
    pooled_all = lax.all_gather(pooled_rows, "tm", axis=0, tiled=False)[:, 0, :]
    owned_mask = (owners == shard_index).astype(jnp.float32)[:, None]
    anchor = summary.astype(jnp.float32) + jnp.take(pooled_all, owners, axis=0).astype(jnp.float32)
    glob_unit, glob_inv = normalize(anchor)
    glob_normed = glob_unit.astype(jnp.bfloat16)
    kv_weights = weights[:, 1:3, :].reshape(width, 2 * local_width)
    glob_kv = jnp.dot(glob_normed, kv_weights, preferred_element_type=jnp.float32).astype(jnp.bfloat16)
    project = weights[:, :3, :].reshape(width, 3 * local_width)
    qkv = jnp.dot(normed, project, preferred_element_type=jnp.float32).astype(jnp.bfloat16)
    keys_local = qkv[:, local_width : 2 * local_width]
    values_local = qkv[:, 2 * local_width :]
    queries = qkv[:, :local_width].reshape(rows_here, heads_here, HEAD_DIM)
    grad_attended = jnp.dot(cotangent, weights[:, 3, :], preferred_element_type=jnp.float32).astype(
        jnp.bfloat16
    )
    grad_attended = grad_attended.reshape(rows_here, heads_here, HEAD_DIM)
    edge = from_behind(qkv[:, local_width:], "tm", 1)
    edge_keys, edge_values = edge[:, :local_width], edge[:, local_width:]
    keys_ext = jnp.concatenate([edge_keys, keys_local], 0).reshape(
        rows_here + WINDOW, heads_here, HEAD_DIM
    )
    values_ext = jnp.concatenate([edge_values, values_local], 0).reshape(
        rows_here + WINDOW, heads_here, HEAD_DIM
    )
    keys_glob = glob_kv[:, :local_width].reshape(glob_count, heads_here, HEAD_DIM)
    values_glob = glob_kv[:, local_width:].reshape(glob_count, heads_here, HEAD_DIM)
    allowed = window_mask(WINDOW, WINDOW, shard_index * rows_here + 0)
    results = block_pass(
        queries, keys_ext, values_ext, keys_glob, values_glob, grad_attended, allowed
    )
    attended = results[0].reshape(rows_here, local_width)
    grad_queries = results[1].reshape(rows_here, local_width)
    grad_kp = results[2].reshape(rows_here + WINDOW, local_width)
    grad_vp = results[3].reshape(rows_here + WINDOW, local_width)
    grad_kg = results[4].reshape(glob_count, local_width)
    grad_vg = results[5].reshape(glob_count, local_width)
    back = from_behind(
        jnp.concatenate([grad_kp[:WINDOW], grad_vp[:WINDOW]], 1).astype(jnp.bfloat16), "tm", -1
    )
    back_keys, back_values = back[:, :local_width], back[:, local_width:]
    grad_keys = grad_kp[WINDOW:].at[rows_here - WINDOW :].add(back_keys.astype(jnp.float32))
    grad_values = grad_vp[WINDOW:].at[rows_here - WINDOW :].add(back_values.astype(jnp.float32))
    grad_cat = jnp.concatenate(
        [grad_queries, grad_keys.astype(jnp.bfloat16), grad_values.astype(jnp.bfloat16)], 1
    )
    glob_grads = jnp.concatenate([grad_kg, grad_vg], 1)
    kv_weights32 = kv_weights.astype(jnp.float32)
    local_features = lax.dot_general(
        glob_grads, kv_weights32, (((1,), (1,)), ((), ())), precision=PRECISE
    )
    glob_cols = to_positions(glob_normed).astype(jnp.float32)
    inner = lax.dot_general(
        to_positions(normed), grad_cat, (((0,), (0,)), ((), ())), preferred_element_type=jnp.float32
    )
    glob_term = lax.dot_general(glob_cols, glob_grads, (((0,), (0,)), ((), ())), precision=PRECISE)
    inner = inner + jnp.concatenate([jnp.zeros((width, local_width), jnp.float32), glob_term], 1)
    last_term = lax.dot_general(
        to_positions(cotangent), attended, (((0,), (0,)), ((), ())), preferred_element_type=jnp.float32
    )
    weight_parts = jnp.concatenate(
        [inner.reshape(width, 3, local_width), last_term.reshape(width, 1, local_width)], 1
    )
    weight_rows, summary_features = butterfly(
        weight_parts.reshape(width, 4 * local_width), local_features, shard_index
    )
    grad_weights = weight_rows.reshape(width // shard_total, 4, local_width)
    grad_summary = norm_back(summary_features, glob_unit, glob_inv)
    pool_grads = lax.dot_general(
        owned_mask, grad_summary, (((0,), (0,)), ((), ())), precision=PRECISE
    )
    mean_grads = norm_back(pool_grads, pool_unit, pool_inv) / rows_here
    half_rows = rows_here // mp_total
    start_row = mp_index * half_rows
    other_row = (1 - mp_index) * half_rows
    feature_all = lax.dot_general(
        grad_cat, project, (((1,), (1,)), ((), ())), preferred_element_type=jnp.float32
    )
    mine = lax.dynamic_slice_in_dim(feature_all, start_row, half_rows, 0)
    theirs = lax.dynamic_slice_in_dim(feature_all, other_row, half_rows, 0).astype(jnp.bfloat16)
    received = lax.ppermute(theirs, "mp", [(0, 1), (1, 0)])
    feature_grads = mine + received.astype(jnp.float32)
    my_unit = lax.dynamic_slice_in_dim(unit_rows, start_row, half_rows, 0)
    my_inverse = lax.dynamic_slice_in_dim(inverse, start_row, half_rows, 0)
    my_cotangent = lax.dynamic_slice_in_dim(cotangent, start_row, half_rows, 0).astype(jnp.float32)
    grad_frames = (
        my_cotangent + norm_back(feature_grads, my_unit, my_inverse) + mean_grads
    ).astype(jnp.bfloat16)
    return (grad_frames, grad_weights, grad_summary)


def solution(mesh):
    in_specs = (P("tm", None), P("tm", None), P(None, None, "mp"), P(), P())
    out_specs = (P(("tm", "mp"), None), P("tm", None, "mp"), P())
    return jax.shard_map(shards, mesh=mesh, in_specs=in_specs, out_specs=out_specs, check_vma=False)
```

profile of v0, /device:TPU:0, one launch (start us, length us, event | category | flops | bytes accessed | tf_op | source)
XLA Modules:
  0.0 347.9 jit_solution(6245019966503695223)
XLA Ops:
  7.2 1.6 convert_reduce_fusion
  9.4 2.8 fusion.32
  12.2 7.1 %copy.76 = bf16[1024,3,512]{0,2,1:T(8,128)(2,1)} copy(bf16[1024,3,512]{2,1,0:T(4,128)(2,1)} %bitcast.128) | data formatting | bytes 6291456
  19.4 3.7 %convolution_convert_fusion = bf16[512,1536]{1,0:T(8,128)(2,1)S(1)} fusion(bf16[512,1024]{1,0:T(8,128)(2,1)S(1)} %get-tuple-element.59, bf16[1024,1536]{0,1:T(8,128)(2,1)} %bitcast.142), kind=kOutput, calls=%fused_computation.16 | convolution fusion | flops 1611399168 | bytes 5767168 | tf_op jit(solution)/shard_map/dot_general | solution.py:208
  24.3 2.3 collective-permute-start
  30.4 6.3 %slice.168 = bf16[1024,2,512]{2,1,0:T(2,128)(2,1)} slice(bf16[1024,4,512]{2,1,0:T(4,128)(2,1)} %param.27), slice={[0:1024], [1:3], [0:512]} | slice | bytes 4194304 | tf_op jit(solution)/shard_map/slice | solution.py:205
  36.7 3.5 %slice.170 = bf16[1024,1,512]{2,1,0:T(2,128)(2,1)} slice(bf16[1024,4,512]{2,1,0:T(4,128)(2,1)S(1)} %copy-done.1), slice={[0:1024], [3:4], [0:512]} | slice | bytes 2097152 | tf_op jit(solution)/shard_map/slice | solution.py:212
  40.2 1.8 copy.70
  49.3 4.8 %copy.78 = bf16[1024,2,512]{0,2,1:T(8,128)(2,1)S(1)} copy(bf16[1024,2,512]{2,1,0:T(2,128)(2,1)} %slice.168) | data formatting | bytes 4194304
  59.1 3.5 convolution_convert_fusion.1
  62.6 1.3 fusion.36
  63.8 2.7 pad_maximum_fusion.2
  66.5 2.3 copy.55
  68.8 2.3 copy.61
  71.1 9.2 %fusion.3 = (f32[8,512]{1,0:T(8,128)}, f32[8,512,1024]{2,1,0:T(8,128)}) fusion(pred[512,1024]{1,0:T(8,128)(4,1)S(1)} %fusion.7, bf16[512,8,64]{0,2,1:T(8,128)(2,1)S(1)} %bitcast.129, bf16[1024,8,64]{0,2,1:T(8,128)(2,1)} %bitcast.134), kind=kOutput, calls=%fused_computation.9 | convolution fusion | flops 549449728 | bytes 18890752 | tf_op jit(solution)/shard_map/qhe,khe->hqk/dot_general | solution.py:137
  80.3 18.4 %all-gather.3.cloned.1.call-done = bf16[512,1024]{1,0:T(8,128)(2,1)} async-done(((bf16[8,1024]{1,0:T(8,128)(2,1)}), bf16[512,1024]{1,0:T(8,128)(2,1)}) %all-gather.3.cloned.1.call-update) | async-done | bytes 1048592 | tf_op jit(solution)/shard_map/all_gather | solution.py:200
  98.7 1.4 slice.208
  103.0 1.6 copy.82
  106.6 8.6 %fusion.4 = f32[8,512]{1,0:T(8,128)} fusion(f32[8,512,1024]{2,1,0:T(8,128)} %get-tuple-element.77, f32[8,512]{1,0:T(8,128)S(1)} %max.8, pred[512,1024]{1,0:T(8,128)(4,1)S(1)} %fusion.7), kind=kLoop, calls=%fused_computation.10 | loop fusion | flops 16773120 | bytes 17334272 | tf_op jit(solution)/shard_map/reduce_sum | solution.py:157
  115.4 1.6 copy.83
  117.7 27.7 %fusion = (f32[8,512]{1,0:T(8,128)S(1)}, bf16[8,512,1024]{2,1,0:T(8,128)(2,1)}, f32[8,512,1024]{2,1,0:T(8,128)}) fusion(f32[8,512]{1,0:T(8,128)S(1)} %add.235, f32[8,512]{1,0:T(8,128)S(1)} %max.8, f32[8,512,1024]{2,1,0:T(8,128)} %get-tuple-element.77, pred[512,1024]{1,0:T(8,128)(4,1)S(1)} %fusion.7, bf16[512,8,64]{0,2,1:T(8,128)(2,1)} %bitcast.144, ...), kind=kOutput, calls=%fused_computation.3 | convolution fusion | flops 570421248 | bytes 44089344 | tf_op jit(solution)/shard_map/qhe,khe->hqk/dot_general | solution.py:137
  145.5 1.3 fusion.10
  146.8 5.2 %convolution_bitcast_fusion = f32[1024,8,64]{0,2,1:T(8,128)S(1)} fusion(bf16[512,8,64]{0,2,1:T(8,128)(2,1)S(1)} %bitcast.147, bf16[8,512,1024]{2,1,0:T(8,128)(2,1)} %get-tuple-element.50), kind=kOutput, calls=%fused_computation.22 | convolution fusion | flops 536870912 | bytes 11010048 | tf_op jit(solution)/shard_map/hqk,qhe->khe/dot_general | solution.py:137
  152.1 8.0 %fusion.2 = bf16[8,512,1024]{2,1,0:T(8,128)(2,1)S(1)} fusion(bf16[8,512,1024]{2,1,0:T(8,128)(2,1)S(1)} %bitcast.123, f32[8,512,1024]{2,1,0:T(8,128)} %get-tuple-element.80, f32[8,512]{1,0:T(8,128)S(1)} %add.236), kind=kLoop, calls=%fused_computation.5 | loop fusion | flops 20971520 | bytes 33570816 | tf_op jit(solution)/shard_map/convert_element_type | solution.py:171
  160.2 1.6 convolution_bitcast_fusion.1
  161.7 1.7 copy-done
  165.4 3.6 %fusion.43 = f32[8,64,512]{2,1,0:T(8,128)} fusion(bf16[1024,8,64]{0,2,1:T(8,128)(2,1)S(1)} %bitcast.139, bf16[8,512,1024]{2,1,0:T(8,128)(2,1)S(1)} %bitcast.123), kind=kOutput, calls=%fused_computation.127 | convolution fusion | flops 536870912 | bytes 10485760 | tf_op jit(solution)/shard_map/hqk,khe->qhe/dot_general | solution.py:137
  171.1 1.3 pad_maximum_fusion.4
  172.4 1.4 collective-permute-start.1
  173.8 1.3 fusion.42
  176.1 2.0 convolution_bitcast_fusion.2
  178.2 6.1 %fusion.40 = f32[8,64,512]{2,1,0:T(8,128)S(1)} fusion(bf16[1024,8,64]{0,2,1:T(8,128)(2,1)S(1)} %bitcast.135, bf16[8,512,1024]{2,1,0:T(8,128)(2,1)} %copy-done), kind=kOutput, calls=%fused_computation.124 | convolution fusion | flops 536870912 | bytes 10485760 | tf_op jit(solution)/shard_map/hqk,khe->qhe/dot_general | solution.py:137
  184.6 1.9 fusion.19
  187.7 4.5 %pad_add_fusion = f32[1024,1536]{1,0:T(8,128)} fusion(f32[1024,1024]{1,0:T(8,128)S(1)} %fusion.19, bf16[512,1024]{0,1:T(8,128)(2,1)S(1)} %bitcast.136, bf16[512,512]{0,1:T(8,128)(2,1)S(1)} %get-tuple-element.69, bf16[512,512]{0,1:T(8,128)(2,1)S(1)} %get-tuple-element.68, bf16[512,512]{0,1:T(8,128)(2,1)S(1)} %bitcast.152), kind=kOutput, calls=%fused_computation.12 | convolution fusion | flops 1616904192 | bytes 13107200 | tf_op jit(solution)/shard_map/dot_general | solution.py:251
  192.2 6.6 %copy.69 = f32[1024,1536]{0,1:T(8,128)} copy(f32[1024,1536]{1,0:T(8,128)} %pad_add_fusion) | data formatting | bytes 12582912 | tf_op jit(solution)/shard_map/add | solution.py:255
  198.8 4.3 %pad_maximum_fusion = f32[1024,4,512]{0,2,1:T(8,128)S(1)} fusion(f32[1024,1,512]{0,2,1:T(8,128)} %convolution_bitcast_fusion.2, f32[1024,3,512]{0,2,1:T(8,128)} %bitcast.125), kind=kLoop, calls=%fused_computation.11 | loop fusion | flops 2097152 | bytes 16777216 | tf_op jit(solution)/shard_map/concatenate | solution.py:259
  203.1 4.3 %constant_dynamic-slice_fusion.6 = (f32[512,2048]{0,1:T(8,128)}, f32[512,2048]{0,1:T(8,128)}) fusion(f32[1024,2048]{0,1:T(8,128)S(1)} %bitcast.124, s32[]{:T(128)S(6)} %select_n.79, s32[]{:T(128)S(6)} %select_n.78), kind=kLoop, calls=%fused_computation.97 | loop fusion | bytes 16777224 | tf_op jit(solution)/shard_map/dynamic_slice | solution.py:118
  207.4 5.4 %copy.81 = f32[512,2048]{1,0:T(8,128)} copy(f32[512,2048]{0,1:T(8,128)} %get-tuple-element.51) | data formatting | bytes 8388608
  212.9 2.4 collective-permute-start.10
  215.2 1.3 fusion.20
  216.7 6.2 %collective-permute-done.3 = f32[64,1024]{1,0:T(8,128)S(1)} collective-permute-done((f32[64,1024]{1,0:T(8,128)S(1)}, f32[64,1024]{1,0:T(8,128)S(1)}, u32[]{:S(2)}, u32[]{:S(2)}) %collective-permute-start.3) | collective-permute-done | bytes 262176 | tf_op jit(solution)/shard_map/ppermute | solution.py:122
  223.0 1.7 collective-permute-start.4
  224.7 4.7 %collective-permute-done.4 = f32[64,1024]{1,0:T(8,128)S(1)} collective-permute-done((f32[64,1024]{1,0:T(8,128)S(1)}, f32[64,1024]{1,0:T(8,128)S(1)}, u32[]{:S(2)}, u32[]{:S(2)}) %collective-permute-start.4) | collective-permute-done | bytes 262176 | tf_op jit(solution)/shard_map/ppermute | solution.py:122
  229.5 4.2 %collective-permute-start.5 = (f32[64,1024]{1,0:T(8,128)S(1)}, f32[64,1024]{1,0:T(8,128)S(1)}, u32[]{:S(2)}, u32[]{:S(2)}) collective-permute-start(f32[64,1024]{1,0:T(8,128)S(1)} %add.244), channel_id=1, source_target_pairs={{0,8},{2,10},{4,12},{6,14},{8,0},{10,2},{12,4},{14,6},{16,24},{18,... | collective-permute-start | bytes 786440 | tf_op jit(solution)/shard_map/ppermute | solution.py:122
  233.7 6.9 %collective-permute-done.5 = f32[64,1024]{1,0:T(8,128)S(1)} collective-permute-done((f32[64,1024]{1,0:T(8,128)S(1)}, f32[64,1024]{1,0:T(8,128)S(1)}, u32[]{:S(2)}, u32[]{:S(2)}) %collective-permute-start.5) | collective-permute-done | bytes 262176 | tf_op jit(solution)/shard_map/ppermute | solution.py:122
  240.6 2.1 collective-permute-start.6
  242.7 7.8 %collective-permute-done.6 = f32[64,1024]{1,0:T(8,128)S(1)} collective-permute-done((f32[64,1024]{1,0:T(8,128)S(1)}, f32[64,1024]{1,0:T(8,128)S(1)}, u32[]{:S(2)}, u32[]{:S(2)}) %collective-permute-start.6) | collective-permute-done | bytes 262176 | tf_op jit(solution)/shard_map/ppermute | solution.py:122
  250.7 2.8 collective-permute-start.7
  253.5 4.0 %fusion.16 = f32[512,1024]{1,0:T(8,128)S(1)} fusion(bf16[1024,1536]{0,1:T(8,128)(2,1)} %bitcast.143, bf16[512,512]{0,1:T(8,128)(2,1)} %copy-done.21, bf16[512,512]{0,1:T(8,128)(2,1)} %copy-done.20, bf16[512,512]{0,1:T(8,128)(2,1)S(1)} %bitcast.153), kind=kOutput, calls=%fused_computation.58 | convolution fusion | flops 1615331328 | bytes 6815744 | tf_op jit(solution)/shard_map/dot_general | solution.py:274
  257.5 1.3 copy-done.12
  272.8 5.5 %copy.80 = f32[512,2048]{1,0:T(8,128)} copy(f32[512,2048]{0,1:T(8,128)} %get-tuple-element.52) | data formatting | bytes 8388608
  279.3 1.5 collective-permute-start.9
  280.8 1.6 multiply_reduce_fusion
  282.5 4.2 %add.257 = f32[512,2048]{1,0:T(8,128)S(1)} add(f32[512,2048]{1,0:T(8,128)} %copy.80, f32[512,2048]{1,0:T(8,128)} %collective-permute-done.10) | non-fusion elementwise | flops 1048576 | bytes 12582912 | tf_op jit(solution)/shard_map/add | solution.py:117
  287.7 2.8 collective-permute-start.11
  291.2 11.6 %collective-permute-done.13 = f32[128,2048]{1,0:T(8,128)S(1)} collective-permute-done((f32[128,2048]{1,0:T(8,128)S(1)}, f32[128,2048]{1,0:T(8,128)S(1)}, u32[]{:S(2)}, u32[]{:S(2)}) %collective-permute-start.13) | collective-permute-done | bytes 1048608 | tf_op jit(solution)/shard_map/ppermute | solution.py:117
  302.8 10.3 %collective-permute-done.12 = f32[128,2048]{1,0:T(8,128)S(1)} collective-permute-done((f32[128,2048]{1,0:T(8,128)S(1)}, f32[128,2048]{1,0:T(8,128)S(1)}, u32[]{:S(2)}, u32[]{:S(2)}) %collective-permute-start.12) | collective-permute-done | bytes 1048608 | tf_op jit(solution)/shard_map/ppermute | solution.py:117
  314.3 3.2 collective-permute-start.16
  318.4 2.4 collective-permute-start.14
  322.1 4.4 %collective-permute-done.16 = f32[32,2048]{1,0:T(8,128)} collective-permute-done((f32[32,2048]{1,0:T(8,128)}, f32[32,2048]{1,0:T(8,128)}, u32[]{:S(2)}, u32[]{:S(2)}) %collective-permute-start.16) | collective-permute-done | bytes 262176 | tf_op jit(solution)/shard_map/ppermute | solution.py:117
  326.5 5.8 %collective-permute-done.15 = f32[32,2048]{1,0:T(8,128)} collective-permute-done((f32[32,2048]{1,0:T(8,128)}, f32[32,2048]{1,0:T(8,128)}, u32[]{:S(2)}, u32[]{:S(2)}) %collective-permute-start.15) | collective-permute-done | bytes 262176 | tf_op jit(solution)/shard_map/ppermute | solution.py:117
  333.5 1.9 collective-permute-start.17
  335.4 2.7 add_convert_fusion
  338.1 2.0 collective-permute-done.17
  (220 shorter events, 43.1 us)
Async XLA Ops:
  7.2 91.5 %all-gather.3.cloned.1.call-start = ((), (), s32[]{:S(2)}) async-start(), calls=%async_computation | async-start | bytes 1064960 | tf_op jit(solution)/shard_map/all_gather | solution.py:200
  8.8 19.8 %copy-start.32 = (f32[1024]{0:T(1024)}, f32[1024]{0:T(1024)S(1)}, u32[]{:S(2)}) copy-start(f32[1024]{0:T(1024)S(1)} %get-tuple-element.43) | copy-start | bytes 12292
  24.3 38.3 %collective-permute-start = (bf16[512,1024]{1,0:T(8,128)(2,1)}, bf16[512,1024]{1,0:T(8,128)(2,1)}, u32[]{:S(2)}, u32[]{:S(2)}) collective-permute-start(bf16[512,1024]{1,0:T(8,128)(2,1)} %slice.204), channel_id=1, source_target_pairs={{0,2},{2,4},{4,6},{6,8},{8,10},{10,12},{12,14},{14,16},{16,18},{18... | collective-permute-start | bytes 3145736 | tf_op jit(solution)/shard_map/ppermute | solution.py:18
  29.2 7.4 %copy-start.1 = (bf16[1024,4,512]{2,1,0:T(4,128)(2,1)S(1)}, bf16[1024,4,512]{2,1,0:T(4,128)(2,1)}, u32[]{:S(2)}) copy-start(bf16[1024,4,512]{2,1,0:T(4,128)(2,1)} %param.27) | copy-start | bytes 12582916
  42.0 4.5 %copy-start.53 = (s32[64]{0:T(128)S(1)}, s32[64]{0:T(128)}, u32[]{:S(2)}) copy-start(s32[64]{0:T(128)} %constant.184.clone) | copy-start | bytes 772
  42.0 5.7 %copy-start.52 = (s32[64]{0:T(128)S(1)}, s32[64]{0:T(128)}, u32[]{:S(2)}) copy-start(s32[64]{0:T(128)} %constant.183.clone) | copy-start | bytes 772
  42.9 6.3 %copy-start.40 = (s32[64]{0:T(128)S(1)}, s32[64]{0:T(128)}, u32[]{:S(2)}) copy-start(s32[64]{0:T(128)} %param.29) | copy-start | bytes 772
  49.2 8.1 %copy-start.23 = (bf16[512,3,2,4,16]{0,4,3,2,1:T(8,128)(2,1)S(1)}, bf16[512,3,2,4,16]{0,4,3,2,1:T(8,128)(2,1)}, u32[]{:S(2)}) copy-start(bf16[512,3,2,4,16]{0,4,3,2,1:T(8,128)(2,1)} %slice.222) | copy-start | bytes 1179652
  49.2 8.1 %copy-start.31 = (bf16[512,1,2,4,16]{0,4,3,2,1:T(8,128)(2,1)S(1)}, bf16[512,1,2,4,16]{0,4,3,2,1:T(8,128)(2,1)}, u32[]{:S(2)}) copy-start(bf16[512,1,2,4,16]{0,4,3,2,1:T(8,128)(2,1)} %slice.221) | copy-start | bytes 393220
  58.6 42.5 %copy-start.36 = (pred[64]{0:T(512)(128)(4,1)}, pred[64]{0:T(512)(128)(4,1)S(1)}, u32[]{:S(2)}) copy-start(pred[64]{0:T(512)(128)(4,1)S(1)} %compare_and_fusion) | copy-start | bytes 196
  71.1 29.7 %copy-start.18 = (bf16[64,1024]{1,0:T(8,128)(2,1)S(1)}, bf16[64,1024]{1,0:T(8,128)(2,1)}, u32[]{:S(2)}) copy-start(bf16[64,1024]{1,0:T(8,128)(2,1)} %param.28) | copy-start | bytes 393220
  101.6 13.6 %copy-start.24 = (bf16[64,1024]{1,0:T(8,128)(2,1)}, bf16[64,1024]{1,0:T(8,128)(2,1)S(1)}, u32[]{:S(2)}) copy-start(bf16[64,1024]{1,0:T(8,128)(2,1)S(1)} %fusion.22) | copy-start | bytes 393220
  105.9 9.3 %copy-start.10 = (f32[8,512,64]{1,2,0:T(8,128)}, f32[8,512,64]{1,2,0:T(8,128)S(1)}, u32[]{:S(2)}) copy-start(f32[8,512,64]{1,2,0:T(8,128)S(1)} %get-tuple-element.79) | copy-start | bytes 3145732
  117.7 27.7 %copy-start.11 = (f32[8,512,64]{1,2,0:T(8,128)S(1)}, f32[8,512,64]{1,2,0:T(8,128)}, u32[]{:S(2)}) copy-start(f32[8,512,64]{1,2,0:T(8,128)} %copy-done.10) | copy-start | bytes 3145732
  117.7 27.7 %copy-start.13 = (bf16[512,512]{0,1:T(8,128)(2,1)S(1)}, bf16[512,512]{0,1:T(8,128)(2,1)}, u32[]{:S(2)}) copy-start(bf16[512,512]{0,1:T(8,128)(2,1)} %convolution_convert_fusion.1) | copy-start | bytes 1572868
  117.7 27.7 %copy-start.29 = (bf16[64,512]{0,1:T(8,128)(2,1)S(1)}, bf16[64,512]{0,1:T(8,128)(2,1)}, u32[]{:S(2)}) copy-start(bf16[64,512]{0,1:T(8,128)(2,1)} %copy.83) | copy-start | bytes 196612
  145.5 6.6 %slice-start = ((s8[8388608]{0:T(1024)(128)(4,1)}), s8[4194304]{0:T(1024)(128)(4,1)S(1)}, s32[]{:S(2)}) async-start(s8[8388608]{0:T(1024)(128)(4,1)} %bitcast.122), calls=%async_computation.1 | async-start | bytes 8388608
  146.8 5.3 %slice-start.1 = ((s8[8388608]{0:T(1024)(128)(4,1)}), s8[4194304]{0:T(1024)(128)(4,1)S(1)}, s32[]{:S(2)}) async-start(s8[8388608]{0:T(1024)(128)(4,1)} %bitcast.122), calls=%async_computation.2 | async-start | bytes 8388608
  152.1 13.2 %copy-start.3 = (f32[1024,8,64]{0,2,1:T(8,128)}, f32[1024,8,64]{0,2,1:T(8,128)S(1)}, u32[]{:S(2)}) copy-start(f32[1024,8,64]{0,2,1:T(8,128)S(1)} %convolution_bitcast_fusion) | copy-start | bytes 6291460
  169.9 5.2 %copy-start.27 = (f32[8,512,64]{1,2,0:T(8,128)S(1)}, f32[8,512,64]{1,2,0:T(8,128)}, u32[]{:S(2)}) copy-start(f32[8,512,64]{1,2,0:T(8,128)} %get-tuple-element.81) | copy-start | bytes 3145732
  169.9 5.7 %copy-start.9 = (f32[8,64,512]{2,1,0:T(8,128)S(1)}, f32[8,64,512]{2,1,0:T(8,128)}, u32[]{:S(2)}) copy-start(f32[8,64,512]{2,1,0:T(8,128)} %fusion.43) | copy-start | bytes 3145732
  169.9 5.7 %copy-start.30 = (bf16[64,512]{0,1:T(8,128)(2,1)S(1)}, bf16[64,512]{0,1:T(8,128)(2,1)}, u32[]{:S(2)}) copy-start(bf16[64,512]{0,1:T(8,128)(2,1)} %copy.83) | copy-start | bytes 196612
  172.4 3.7 %copy-start.7 = (bf16[512,2,2,2,2,2,2,16]{0,7,6,5,4,3,2,1:T(8,128)(2,1)S(1)}, bf16[512,2,2,2,2,2,2,16]{0,7,6,5,4,3,2,1:T(8,128)(2,1)}, u32[]{:S(2)}) copy-start(bf16[512,2,2,2,2,2,2,16]{0,7,6,5,4,3,2,1:T(8,128)(2,1)} %copy.71) | copy-start | bytes 3145732
  172.4 14.1 %collective-permute-start.1 = (bf16[512,1024]{0,1:T(8,128)(2,1)S(1)}, bf16[512,1024]{0,1:T(8,128)(2,1)S(1)}, u32[]{:S(2)}, u32[]{:S(2)}) collective-permute-start(bf16[512,1024]{0,1:T(8,128)(2,1)S(1)} %pad_maximum_fusion.4), channel_id=1, source_target_pairs={{2,0},{4,2},{6,4},{8,6},{10,8},{12,10},{14,12},{16,14},{18,16},{20... | collective-permute-start | bytes 3145736 | tf_op jit(solution)/shard_map/ppermute | solution.py:18
  175.1 9.4 %copy-start.14 = (f32[8,64,64]{2,1,0:T(8,128)}, f32[8,64,64]{2,1,0:T(8,128)S(1)}, u32[]{:S(2)}) copy-start(f32[8,64,64]{2,1,0:T(8,128)S(1)} %fusion.42) | copy-start | bytes 393220
  175.7 8.9 %copy-start.16 = (f32[8,64,64]{2,1,0:T(8,128)}, f32[8,64,64]{2,1,0:T(8,128)S(1)}, u32[]{:S(2)}) copy-start(f32[8,64,64]{2,1,0:T(8,128)S(1)} %fusion.41) | copy-start | bytes 393220
  178.2 6.1 %copy-start.26 = (bf16[64,512]{0,1:T(8,128)(2,1)S(1)}, bf16[64,512]{0,1:T(8,128)(2,1)}, u32[]{:S(2)}) copy-start(bf16[64,512]{0,1:T(8,128)(2,1)} %copy.82) | copy-start | bytes 196612
  186.9 5.3 %copy-start.20 = (bf16[512,512]{0,1:T(8,128)(2,1)}, bf16[512,512]{0,1:T(8,128)(2,1)S(1)}, u32[]{:S(2)}) copy-start(bf16[512,512]{0,1:T(8,128)(2,1)S(1)} %get-tuple-element.68) | copy-start | bytes 1572868
  207.4 7.8 %copy-start.15 = (f32[8,64,64]{2,1,0:T(8,128)S(1)}, f32[8,64,64]{2,1,0:T(8,128)}, u32[]{:S(2)}) copy-start(f32[8,64,64]{2,1,0:T(8,128)} %copy-done.14) | copy-start | bytes 393220
  207.4 7.8 %copy-start.17 = (f32[8,64,64]{2,1,0:T(8,128)S(1)}, f32[8,64,64]{2,1,0:T(8,128)}, u32[]{:S(2)}) copy-start(f32[8,64,64]{2,1,0:T(8,128)} %copy-done.16) | copy-start | bytes 393220
  212.9 69.6 %collective-permute-start.10 = (f32[512,2048]{1,0:T(8,128)}, f32[512,2048]{1,0:T(8,128)}, u32[]{:S(2)}, u32[]{:S(2)}) collective-permute-start(f32[512,2048]{1,0:T(8,128)} %copy.81), channel_id=1, source_target_pairs={{0,2},{2,0},{4,6},{6,4},{8,10},{10,8},{12,14},{14,12},{16,18},{18,... | collective-permute-start | bytes 12582920 | tf_op jit(solution)/shard_map/ppermute | solution.py:117
  216.5 6.5 %collective-permute-start.3 = (f32[64,1024]{1,0:T(8,128)S(1)}, f32[64,1024]{1,0:T(8,128)S(1)}, u32[]{:S(2)}, u32[]{:S(2)}) collective-permute-start(f32[64,1024]{1,0:T(8,128)S(1)} %fusion.20), channel_id=1, source_target_pairs={{0,4},{2,14},{4,0},{6,10},{8,12},{10,6},{12,8},{14,2},{16,20},{18,... | collective-permute-start | bytes 786440 | tf_op jit(solution)/shard_map/ppermute | solution.py:122
  223.0 6.5 %collective-permute-start.4 = (f32[64,1024]{1,0:T(8,128)S(1)}, f32[64,1024]{1,0:T(8,128)S(1)}, u32[]{:S(2)}, u32[]{:S(2)}) collective-permute-start(f32[64,1024]{1,0:T(8,128)S(1)} %add.243), channel_id=1, source_target_pairs={{0,32},{2,98},{4,36},{6,102},{8,40},{10,106},{12,44},{14,110},{16,... | collective-permute-start | bytes 786440 | tf_op jit(solution)/shard_map/ppermute | solution.py:122
  229.5 11.0 %collective-permute-start.5 = (f32[64,1024]{1,0:T(8,128)S(1)}, f32[64,1024]{1,0:T(8,128)S(1)}, u32[]{:S(2)}, u32[]{:S(2)}) collective-permute-start(f32[64,1024]{1,0:T(8,128)S(1)} %add.244), channel_id=1, source_target_pairs={{0,8},{2,10},{4,12},{6,14},{8,0},{10,2},{12,4},{14,6},{16,24},{18,... | collective-permute-start | bytes 786440 | tf_op jit(solution)/shard_map/ppermute | solution.py:122
  240.6 9.9 %collective-permute-start.6 = (f32[64,1024]{1,0:T(8,128)S(1)}, f32[64,1024]{1,0:T(8,128)S(1)}, u32[]{:S(2)}, u32[]{:S(2)}) collective-permute-start(f32[64,1024]{1,0:T(8,128)S(1)} %add.245), channel_id=1, source_target_pairs={{0,64},{2,66},{4,68},{6,70},{8,72},{10,74},{12,76},{14,78},{16,80}... | collective-permute-start | bytes 786440 | tf_op jit(solution)/shard_map/ppermute | solution.py:122
  250.5 9.9 %copy-start.51 = (s32[64]{0:T(128)S(1)}, s32[64]{0:T(128)}, u32[]{:S(2)}) copy-start(s32[64]{0:T(128)} %constant.186.clone) | copy-start | bytes 772
  250.5 11.2 %copy-start.50 = (s32[64]{0:T(128)S(1)}, s32[64]{0:T(128)}, u32[]{:S(2)}) copy-start(s32[64]{0:T(128)} %constant.188.clone) | copy-start | bytes 772
  250.5 12.4 %copy-start.49 = (s32[64]{0:T(128)S(1)}, s32[64]{0:T(128)}, u32[]{:S(2)}) copy-start(s32[64]{0:T(128)} %constant.187.clone) | copy-start | bytes 772
  250.6 13.6 %copy-start.48 = (s32[64]{0:T(128)S(1)}, s32[64]{0:T(128)}, u32[]{:S(2)}) copy-start(s32[64]{0:T(128)} %constant.185.clone) | copy-start | bytes 772
  250.6 14.7 %copy-start.47 = (s32[64]{0:T(128)S(1)}, s32[64]{0:T(128)}, u32[]{:S(2)}) copy-start(s32[64]{0:T(128)} %constant.190.clone) | copy-start | bytes 772
  250.6 15.9 %copy-start.46 = (s32[64]{0:T(128)S(1)}, s32[64]{0:T(128)}, u32[]{:S(2)}) copy-start(s32[64]{0:T(128)} %constant.192.clone) | copy-start | bytes 772
  250.6 17.0 %copy-start.45 = (s32[64]{0:T(128)S(1)}, s32[64]{0:T(128)}, u32[]{:S(2)}) copy-start(s32[64]{0:T(128)} %constant.191.clone) | copy-start | bytes 772
  250.6 18.3 %copy-start.44 = (s32[64]{0:T(128)S(1)}, s32[64]{0:T(128)}, u32[]{:S(2)}) copy-start(s32[64]{0:T(128)} %constant.189.clone) | copy-start | bytes 772
  250.6 19.4 %copy-start.43 = (s32[64]{0:T(128)S(1)}, s32[64]{0:T(128)}, u32[]{:S(2)}) copy-start(s32[64]{0:T(128)} %constant.194.clone) | copy-start | bytes 772
  250.6 20.7 %copy-start.42 = (s32[64]{0:T(128)S(1)}, s32[64]{0:T(128)}, u32[]{:S(2)}) copy-start(s32[64]{0:T(128)} %constant.193.clone) | copy-start | bytes 772
  250.6 22.0 %copy-start.35 = (f32[512]{0:T(512)S(1)}, f32[512]{0:T(512)}, u32[]{:S(2)}) copy-start(f32[512]{0:T(512)} %copy-done.34) | copy-start | bytes 6148
  250.7 9.7 %collective-permute-start.7 = (f32[64,1024]{1,0:T(8,128)S(1)}, f32[64,1024]{1,0:T(8,128)S(1)}, u32[]{:S(2)}, u32[]{:S(2)}) collective-permute-start(f32[64,1024]{1,0:T(8,128)S(1)} %add.246), channel_id=1, source_target_pairs={{0,16},{2,18},{4,20},{6,22},{8,24},{10,26},{12,28},{14,30},{16,0},... | collective-permute-start | bytes 786440 | tf_op jit(solution)/shard_map/ppermute | solution.py:122
  259.7 21.1 %collective-permute-start.2 = (bf16[256,1024]{1,0:T(8,128)(2,1)}, bf16[256,1024]{1,0:T(8,128)(2,1)S(1)}, u32[]{:S(2)}, u32[]{:S(2)}) collective-permute-start(bf16[256,1024]{1,0:T(8,128)(2,1)} %dynamic-slice_convert_fusion), channel_id=1, source_target_pairs={{0,1},{1,0},{2,3},{3,2},{4,5},{5,4},{6,7},{7,6},{8,9},{9,8},{10,11... | collective-permute-start | bytes 1572872 | tf_op jit(solution)/shard_map/ppermute | solution.py:279
  260.4 18.0 %collective-permute-start.8 = (f32[64,1024]{1,0:T(8,128)S(1)}, f32[64,1024]{1,0:T(8,128)}, u32[]{:S(2)}, u32[]{:S(2)}) collective-permute-start(f32[64,1024]{1,0:T(8,128)S(1)} %add.247), channel_id=1, source_target_pairs={{0,2},{2,0},{4,6},{6,4},{8,10},{10,8},{12,14},{14,12},{16,18},{18,... | collective-permute-start | bytes 786440 | tf_op jit(solution)/shard_map/ppermute | solution.py:122
  272.8 8.1 %copy-start.4 = (f32[512,1024]{1,0:T(8,128)S(1)}, f32[512,1024]{1,0:T(8,128)}, u32[]{:S(2)}) copy-start(f32[512,1024]{1,0:T(8,128)} %get-tuple-element.60) | copy-start | bytes 6291460
  279.3 11.2 %collective-permute-start.9 = (f32[64,1024]{1,0:T(8,128)S(1)}, f32[64,1024]{1,0:T(8,128)S(1)}, u32[]{:S(2)}, u32[]{:S(2)}) collective-permute-start(f32[64,1024]{1,0:T(8,128)S(1)} %add.248), channel_id=1, source_target_pairs={{0,1},{1,0},{2,3},{3,2},{4,5},{5,4},{6,7},{7,6},{8,9},{9,8},{10,11... | collective-permute-start | bytes 786440 | tf_op jit(solution)/shard_map/ppermute | solution.py:123
  280.8 5.9 %copy-start.19 = (bf16[256,1024]{1,0:T(8,128)(2,1)}, bf16[256,1024]{1,0:T(8,128)(2,1)S(1)}, u32[]{:S(2)}) copy-start(bf16[256,1024]{1,0:T(8,128)(2,1)S(1)} %collective-permute-done.2) | copy-start | bytes 1572868
  286.7 3.8 %copy-start.37 = (pred[64]{0:T(512)(128)(4,1)S(1)}, pred[64]{0:T(512)(128)(4,1)}, u32[]{:S(2)}) copy-start(pred[64]{0:T(512)(128)(4,1)} %copy-done.36) | copy-start | bytes 196
  286.7 3.8 %copy-start.39 = (f32[64]{0:T(128)S(1)}, f32[64]{0:T(128)}, u32[]{:S(2)}) copy-start(f32[64]{0:T(128)} %copy-done.38) | copy-start | bytes 772
  286.7 4.2 %copy-start.41 = (s32[64]{0:T(128)S(1)}, s32[64]{0:T(128)}, u32[]{:S(2)}) copy-start(s32[64]{0:T(128)} %param.29) | copy-start | bytes 772
  287.0 15.9 %collective-permute-start.13 = (f32[128,2048]{1,0:T(8,128)S(1)}, f32[128,2048]{1,0:T(8,128)S(1)}, u32[]{:S(2)}, u32[]{:S(2)}) collective-permute-start(f32[128,2048]{1,0:T(8,128)S(1)} %get-tuple-element.54), channel_id=1, source_target_pairs={{0,36},{2,110},{4,32},{6,106},{8,44},{10,102},{12,40},{14,98},{16,... | collective-permute-start | bytes 3145736 | tf_op jit(solution)/shard_map/ppermute | solution.py:117
  287.1 26.1 %collective-permute-start.12 = (f32[128,2048]{1,0:T(8,128)S(1)}, f32[128,2048]{1,0:T(8,128)S(1)}, u32[]{:S(2)}, u32[]{:S(2)}) collective-permute-start(f32[128,2048]{1,0:T(8,128)S(1)} %get-tuple-element.55), channel_id=1, source_target_pairs={{0,4},{2,14},{4,0},{6,10},{8,12},{10,6},{12,8},{14,2},{16,20},{18,... | collective-permute-start | bytes 3145736 | tf_op jit(solution)/shard_map/ppermute | solution.py:117
  287.7 25.5 %collective-permute-start.11 = (f32[128,2048]{1,0:T(8,128)S(1)}, f32[128,2048]{1,0:T(8,128)S(1)}, u32[]{:S(2)}, u32[]{:S(2)}) collective-permute-start(f32[128,2048]{1,0:T(8,128)S(1)} %get-tuple-element.53), channel_id=1, source_target_pairs={{0,32},{2,98},{4,36},{6,102},{8,40},{10,106},{12,44},{14,110},{16,... | collective-permute-start | bytes 3145736 | tf_op jit(solution)/shard_map/ppermute | solution.py:117
  290.8 30.0 %copy-start.33 = (f32[1024]{0:T(1024)S(1)}, f32[1024]{0:T(1024)}, u32[]{:S(2)}) copy-start(f32[1024]{0:T(1024)} %copy-done.32) | copy-start | bytes 12292
  291.0 22.2 %copy-start.28 = (f32[64,1024]{1,0:T(8,128)}, f32[64,1024]{1,0:T(8,128)S(1)}, u32[]{:S(2)}) copy-start(f32[64,1024]{1,0:T(8,128)S(1)} %subtract_multiply_fusion) | copy-start | bytes 786436
  314.3 12.1 %collective-permute-start.16 = (f32[32,2048]{1,0:T(8,128)}, f32[32,2048]{1,0:T(8,128)}, u32[]{:S(2)}, u32[]{:S(2)}) collective-permute-start(f32[32,2048]{1,0:T(8,128)} %get-tuple-element.62), channel_id=1, source_target_pairs={{0,72},{2,74},{4,76},{6,78},{8,64},{10,66},{12,68},{14,70},{16,88}... | collective-permute-start | bytes 786440 | tf_op jit(solution)/shard_map/ppermute | solution.py:117
  317.6 14.7 %collective-permute-start.15 = (f32[32,2048]{1,0:T(8,128)}, f32[32,2048]{1,0:T(8,128)}, u32[]{:S(2)}, u32[]{:S(2)}) collective-permute-start(f32[32,2048]{1,0:T(8,128)} %get-tuple-element.63), channel_id=1, source_target_pairs={{0,8},{2,10},{4,12},{6,14},{8,0},{10,2},{12,4},{14,6},{16,24},{18,... | collective-permute-start | bytes 786440 | tf_op jit(solution)/shard_map/ppermute | solution.py:117
  318.4 13.9 %collective-permute-start.14 = (f32[32,2048]{1,0:T(8,128)S(1)}, f32[32,2048]{1,0:T(8,128)}, u32[]{:S(2)}, u32[]{:S(2)}) collective-permute-start(f32[32,2048]{1,0:T(8,128)S(1)} %get-tuple-element.61), channel_id=1, source_target_pairs={{0,64},{2,66},{4,68},{6,70},{8,72},{10,74},{12,76},{14,78},{16,80}... | collective-permute-start | bytes 786440 | tf_op jit(solution)/shard_map/ppermute | solution.py:117
  333.5 6.6 %collective-permute-start.17 = (f32[16,2048]{1,0:T(8,128)S(1)}, f32[16,2048]{1,0:T(8,128)S(1)}, u32[]{:S(2)}, u32[]{:S(2)}) collective-permute-start(f32[16,2048]{1,0:T(8,128)S(1)} %constant_dynamic-slice_fusion.8), channel_id=1, source_target_pairs={{0,16},{2,18},{4,20},{6,22},{8,24},{10,26},{12,28},{14,30},{16,0},... | collective-permute-start | bytes 393224 | tf_op jit(solution)/shard_map/ppermute | solution.py:117
  (13 other events, 27.7 us)
Sparse Core Ops, SparseCore 0:
  29.3 69.2 all-gather.2
where the time goes:
time: 349 us; the launch traced here: 348 us
  local copies, waits for them, and re-layouts  86.2 us (25%)
  matrix products  80.1 us (23%)
  waiting for transfers between devices  78.2 us (22%)
  other arithmetic  48.1 us (14%)
  starting transfers between devices  31.3 us (9%)
  between operations  24 us (7%)
    dot_general x12, matrix products, product(): return jnp.einsum(form, left, right, preferred_element_type=jnp.float32)  58.2 us
    ppermute x8, waiting for transfers between devices, butterfly(): lax.ppermute(lax.dynamic_slice_in_dim(parts, sent * size, size, 0), 'tm',...  34.2 us
    unnamed x118, local copies, waits for them, and re-layouts  30.1 us
    ppermute x6, waiting for transfers between devices, butterfly(): glob = glob + lax.ppermute(glob, 'tm', pairs)  25.6 us
    all_gather x1, waiting for transfers between devices, shards(): pooled_all = lax.all_gather(pooled_rows, 'tm', axis=0, tiled=False)[:, 0, :]  18.4 us
    ppermute x8, starting transfers between devices, butterfly(): lax.ppermute(lax.dynamic_slice_in_dim(parts, sent * size, size, 0), 'tm',...  14.4 us
    ppermute x6, starting transfers between devices, butterfly(): glob = glob + lax.ppermute(glob, 'tm', pairs)  11.1 us
    reduce_sum x1, other arithmetic, block_pass(): jnp.sum(near_exp, axis=-1, keepdims=True)  8.57 us
  transfers between devices with their start and end apart: 19, of which 10 were waited for; matrix products, arithmetic and copies ran while one was open for 27% of the time, Pallas kernels for 0%

commit v1 on v0

--- a/solution.py
+++ b/solution.py
@@ -94,17 +94,26 @@
     return steps
 
 
-def glob_rounds():
-    rounds = []
-    for flip in ((1, 0), (0, 1), (2, 0), (0, 2)):
-        pairs = []
+def glob_steps():
+    steps = []
+    for mask, shift in ((1, 0), (2, 1)):
+        slots = np.zeros(64, np.int32)
         for i in range(64):
             core, zl, xl, y_half = labels(i)
-            pairs.append((i, from_labels(core, zl ^ flip[0], xl ^ flip[1], y_half)))
-        rounds.append(pairs)
-    rounds.append([(i, i ^ 8) for i in range(64)])
-    rounds.append([(i, i ^ 1) for i in range(64)])
-    return rounds
+            slots[i] = ((zl & mask) >> shift) * 2 + ((xl & mask) >> shift)
+        partners = []
+        for d in (1, 2, 3):
+            pairs = []
+            for i in range(64):
+                core, zl, xl, y_half = labels(i)
+                zl ^= mask if d & 2 else 0
+                xl ^= mask if d & 1 else 0
+                pairs.append((i, from_labels(core, zl, xl, y_half)))
+            partners.append(pairs)
+        steps.append((slots, partners))
+    slots = np.array([((i >> 3) & 1) * 2 + (i & 1) for i in range(64)], np.int32)
+    steps.append((slots, [[(i, i ^ flip) for i in range(64)] for flip in (1, 8, 9)]))
+    return steps
 
 
 def butterfly(parts, glob, shard_index):
@@ -118,8 +127,11 @@
                 lax.dynamic_slice_in_dim(parts, sent * size, size, 0), "tm", pairs
             )
         parts = total
-    for pairs in glob_rounds():
-        glob = glob + lax.ppermute(glob, "tm", pairs)
+    for slot_table, partners in glob_steps():
+        slot = jnp.asarray(slot_table)[shard_index]
+        held = jnp.stack([glob] + [lax.ppermute(glob, "tm", pairs) for pairs in partners])
+        ordered = [lax.dynamic_index_in_dim(held, slot ^ s, 0, keepdims=False) for s in range(4)]
+        glob = (ordered[0] + ordered[1]) + (ordered[2] + ordered[3])
     glob = glob + lax.ppermute(glob, "mp", [(0, 1), (1, 0)])
     return parts, glob
 

time: 349 us -> 351 us (level)
  waiting for transfers between devices: 78.2 us -> 64.8 us
  between operations: 24 us -> 36 us
  starting transfers between devices: 31.3 us -> 35.9 us
    ppermute x6 -> x9, waiting for transfers between devices: 25.6 us -> 16.9 us  [butterfly(): lax.ppermute(glob, 'tm', pairs)]
    ppermute x8, waiting for transfers between devices: 34.2 us -> 29.5 us  [butterfly(): lax.ppermute(lax.dynamic_slice_in_dim(parts, sent * size, size, 0), 'tm',...]
    ppermute x6 -> x9, starting transfers between devices: 11.1 us -> 14.6 us  [butterfly(): lax.ppermute(glob, 'tm', pairs)]
    unnamed x118 -> x124, local copies, waits for them, and re-layouts: 30.1 us -> 29.8 us
  transfers between devices with their start and end apart: 19 -> 22, of which waited for: 10 -> 11; matrix products, arithmetic and copies ran while one was open for 27% -> 25% of each run, Pallas kernels for 0% -> 0%
where the time goes in v1:
time: 351 us; the launch traced here: 349 us
  local copies, waits for them, and re-layouts  86.7 us (25%)
  matrix products  79.1 us (23%)
  waiting for transfers between devices  64.8 us (18%)
  other arithmetic  46.5 us (13%)
  between operations  36 us (10%)
  starting transfers between devices  35.9 us (10%)
    dot_general x12, matrix products, product(): return jnp.einsum(form, left, right, preferred_element_type=jnp.float32)  58.1 us
    unnamed x124, local copies, waits for them, and re-layouts  29.8 us
    ppermute x8, waiting for transfers between devices, butterfly(): lax.ppermute(lax.dynamic_slice_in_dim(parts, sent * size, size, 0), 'tm',...  29.5 us
    all_gather x1, waiting for transfers between devices, shards(): pooled_all = lax.all_gather(pooled_rows, 'tm', axis=0, tiled=False)[:, 0, :]  18.4 us
    ppermute x9, waiting for transfers between devices, butterfly(): lax.ppermute(glob, 'tm', pairs)  16.9 us
    ppermute x8, starting transfers between devices, butterfly(): lax.ppermute(lax.dynamic_slice_in_dim(parts, sent * size, size, 0), 'tm',...  15.5 us
    ppermute x9, starting transfers between devices, butterfly(): lax.ppermute(glob, 'tm', pairs)  14.6 us
    reduce_sum x1, other arithmetic, block_pass(): jnp.sum(near_exp, axis=-1, keepdims=True)  8.57 us
  transfers between devices with their start and end apart: 22, of which 11 were waited for; matrix products, arithmetic and copies ran while one was open for 25% of the time, Pallas kernels for 0%

profile of v1, /device:TPU:0, one launch (start us, length us, event | category | flops | bytes accessed | tf_op | source)
XLA Modules:
  0.0 349.1 jit_solution(7636870169152392752)
XLA Ops:
  7.2 1.6 convert_reduce_fusion
  9.4 2.8 fusion.32
  12.2 7.1 %copy.79 = bf16[1024,3,512]{0,2,1:T(8,128)(2,1)} copy(bf16[1024,3,512]{2,1,0:T(4,128)(2,1)} %bitcast.149) | data formatting | bytes 6291456
  19.4 3.7 %convolution_convert_fusion = bf16[512,1536]{1,0:T(8,128)(2,1)S(1)} fusion(bf16[512,1024]{1,0:T(8,128)(2,1)S(1)} %get-tuple-element.59, bf16[1024,1536]{0,1:T(8,128)(2,1)} %bitcast.163), kind=kOutput, calls=%fused_computation.16 | convolution fusion | flops 1611399168 | bytes 5767168 | tf_op jit(solution)/shard_map/dot_general | solution.py:220
  24.3 2.3 collective-permute-start
  30.4 6.2 %slice.168 = bf16[1024,2,512]{2,1,0:T(2,128)(2,1)} slice(bf16[1024,4,512]{2,1,0:T(4,128)(2,1)} %param.30), slice={[0:1024], [1:3], [0:512]} | slice | bytes 4194304 | tf_op jit(solution)/shard_map/slice | solution.py:217
  36.6 3.5 slice.170
  40.1 1.8 copy.73
  49.3 4.8 %copy.81 = bf16[1024,2,512]{0,2,1:T(8,128)(2,1)S(1)} copy(bf16[1024,2,512]{2,1,0:T(2,128)(2,1)} %slice.168) | data formatting | bytes 4194304
  59.1 3.5 convolution_convert_fusion.1
  62.6 1.3 fusion.36
  63.9 2.7 pad_maximum_fusion.2
  66.5 2.3 copy.58
  68.8 2.3 copy.64
  71.1 9.2 %fusion.3 = (f32[8,512]{1,0:T(8,128)}, f32[8,512,1024]{2,1,0:T(8,128)}) fusion(pred[512,1024]{1,0:T(8,128)(4,1)S(1)} %fusion.7, bf16[512,8,64]{0,2,1:T(8,128)(2,1)S(1)} %bitcast.150, bf16[1024,8,64]{0,2,1:T(8,128)(2,1)} %bitcast.155), kind=kOutput, calls=%fused_computation.9 | convolution fusion | flops 549449728 | bytes 18890752 | tf_op jit(solution)/shard_map/qhe,khe->hqk/dot_general | solution.py:149
  80.3 18.4 %all-gather.3.cloned.1.call-done = bf16[512,1024]{1,0:T(8,128)(2,1)} async-done(((bf16[8,1024]{1,0:T(8,128)(2,1)}), bf16[512,1024]{1,0:T(8,128)(2,1)}) %all-gather.3.cloned.1.call-update) | async-done | bytes 1048592 | tf_op jit(solution)/shard_map/all_gather | solution.py:212
  98.7 1.4 slice.208
  103.0 1.6 copy.85
  106.6 8.6 %fusion.4 = f32[8,512]{1,0:T(8,128)} fusion(f32[8,512,1024]{2,1,0:T(8,128)} %get-tuple-element.77, f32[8,512]{1,0:T(8,128)S(1)} %max.8, pred[512,1024]{1,0:T(8,128)(4,1)S(1)} %fusion.7), kind=kLoop, calls=%fused_computation.10 | loop fusion | flops 16773120 | bytes 17334272 | tf_op jit(solution)/shard_map/reduce_sum | solution.py:169
  115.4 1.6 copy.86
  117.7 27.6 %fusion = (f32[8,512]{1,0:T(8,128)S(1)}, bf16[8,512,1024]{2,1,0:T(8,128)(2,1)}, f32[8,512,1024]{2,1,0:T(8,128)}) fusion(f32[8,512]{1,0:T(8,128)S(1)} %add.305, f32[8,512]{1,0:T(8,128)S(1)} %max.8, f32[8,512,1024]{2,1,0:T(8,128)} %get-tuple-element.77, pred[512,1024]{1,0:T(8,128)(4,1)S(1)} %fusion.7, bf16[512,8,64]{0,2,1:T(8,128)(2,1)} %bitcast.165, ...), kind=kOutput, calls=%fused_computation.3 | convolution fusion | flops 570421248 | bytes 44089344 | tf_op jit(solution)/shard_map/qhe,khe->hqk/dot_general | solution.py:149
  145.4 1.3 fusion.10
  146.8 5.2 %convolution_bitcast_fusion = f32[1024,8,64]{0,2,1:T(8,128)S(1)} fusion(bf16[512,8,64]{0,2,1:T(8,128)(2,1)S(1)} %bitcast.168, bf16[8,512,1024]{2,1,0:T(8,128)(2,1)} %get-tuple-element.50), kind=kOutput, calls=%fused_computation.22 | convolution fusion | flops 536870912 | bytes 11010048 | tf_op jit(solution)/shard_map/hqk,qhe->khe/dot_general | solution.py:149
  152.1 8.0 %fusion.2 = bf16[8,512,1024]{2,1,0:T(8,128)(2,1)S(1)} fusion(bf16[8,512,1024]{2,1,0:T(8,128)(2,1)S(1)} %bitcast.144, f32[8,512,1024]{2,1,0:T(8,128)} %get-tuple-element.80, f32[8,512]{1,0:T(8,128)S(1)} %add.306), kind=kLoop, calls=%fused_computation.5 | loop fusion | flops 20971520 | bytes 33570816 | tf_op jit(solution)/shard_map/convert_element_type | solution.py:183
  160.1 1.6 convolution_bitcast_fusion.1
  161.7 1.7 copy-done
  165.4 3.7 %fusion.43 = f32[8,64,512]{2,1,0:T(8,128)} fusion(bf16[1024,8,64]{0,2,1:T(8,128)(2,1)S(1)} %bitcast.160, bf16[8,512,1024]{2,1,0:T(8,128)(2,1)S(1)} %bitcast.144), kind=kOutput, calls=%fused_computation.133 | convolution fusion | flops 536870912 | bytes 10485760 | tf_op jit(solution)/shard_map/hqk,khe->qhe/dot_general | solution.py:149
  171.0 1.3 pad_maximum_fusion.4
  172.3 1.4 collective-permute-start.1
  173.8 1.3 fusion.42
  176.0 2.0 convolution_bitcast_fusion.2
  178.1 6.1 %fusion.40 = f32[8,64,512]{2,1,0:T(8,128)S(1)} fusion(bf16[1024,8,64]{0,2,1:T(8,128)(2,1)S(1)} %bitcast.156, bf16[8,512,1024]{2,1,0:T(8,128)(2,1)} %copy-done), kind=kOutput, calls=%fused_computation.130 | convolution fusion | flops 536870912 | bytes 10485760 | tf_op jit(solution)/shard_map/hqk,khe->qhe/dot_general | solution.py:149
  184.5 1.9 fusion.19
  186.9 4.6 %pad_add_fusion = f32[1024,1536]{1,0:T(8,128)} fusion(f32[1024,1024]{1,0:T(8,128)S(1)} %fusion.19, bf16[512,1024]{0,1:T(8,128)(2,1)S(1)} %bitcast.157, bf16[512,512]{0,1:T(8,128)(2,1)S(1)} %get-tuple-element.69, bf16[512,512]{0,1:T(8,128)(2,1)S(1)} %get-tuple-element.68, bf16[512,512]{0,1:T(8,128)(2,1)S(1)} %bitcast.173), kind=kOutput, calls=%fused_computation.12 | convolution fusion | flops 1616904192 | bytes 13107200 | tf_op jit(solution)/shard_map/dot_general | solution.py:263
  191.4 6.6 %copy.72 = f32[1024,1536]{0,1:T(8,128)} copy(f32[1024,1536]{1,0:T(8,128)} %pad_add_fusion) | data formatting | bytes 12582912 | tf_op jit(solution)/shard_map/add | solution.py:267
  198.0 4.3 %pad_maximum_fusion = f32[1024,4,512]{0,2,1:T(8,128)S(1)} fusion(f32[1024,1,512]{0,2,1:T(8,128)} %convolution_bitcast_fusion.2, f32[1024,3,512]{0,2,1:T(8,128)} %bitcast.146), kind=kLoop, calls=%fused_computation.11 | loop fusion | flops 2097152 | bytes 16777216 | tf_op jit(solution)/shard_map/concatenate | solution.py:271
  202.3 4.2 %constant_dynamic-slice_fusion.3 = (f32[512,2048]{0,1:T(8,128)}, f32[512,2048]{0,1:T(8,128)}) fusion(f32[1024,2048]{0,1:T(8,128)S(1)} %bitcast.145, s32[]{:T(128)S(6)} %select_n.131, s32[]{:T(128)S(6)} %select_n.130), kind=kLoop, calls=%fused_computation.95 | loop fusion | bytes 16777224 | tf_op jit(solution)/shard_map/dynamic_slice | solution.py:127
  206.6 5.5 %copy.84 = f32[512,2048]{1,0:T(8,128)} copy(f32[512,2048]{0,1:T(8,128)} %get-tuple-element.51) | data formatting | bytes 8388608
  212.1 2.4 collective-permute-start.13
  216.1 2.9 collective-permute-start.4
  223.8 2.1 collective-permute-done.4
  226.1 6.7 %collective-permute-start.8 = (f32[64,1024]{1,0:T(8,128)S(1)}, f32[64,1024]{1,0:T(8,128)S(1)}, u32[]{:S(2)}, u32[]{:S(2)}) collective-permute-start(f32[64,1024]{1,0:T(8,128)S(1)} %fusion.81), channel_id=1, source_target_pairs={{0,72},{2,74},{4,76},{6,78},{8,64},{10,66},{12,68},{14,70},{16,88}... | collective-permute-start | bytes 786440 | tf_op jit(solution)/shard_map/ppermute | solution.py:132
  238.6 6.9 %collective-permute-done.7 = f32[64,1024]{1,0:T(8,128)S(1)} collective-permute-done((f32[64,1024]{1,0:T(8,128)S(1)}, f32[64,1024]{1,0:T(8,128)S(1)}, u32[]{:S(2)}, u32[]{:S(2)}) %collective-permute-start.7) | collective-permute-done | bytes 262176 | tf_op jit(solution)/shard_map/ppermute | solution.py:132
  245.7 1.3 collective-permute-start.11
  247.0 1.9 collective-permute-start.10
  254.0 1.8 collective-permute-done.11
  255.8 5.8 %collective-permute-done.10 = f32[64,1024]{1,0:T(8,128)S(1)} collective-permute-done((f32[64,1024]{1,0:T(8,128)S(1)}, f32[64,1024]{1,0:T(8,128)S(1)}, u32[]{:S(2)}, u32[]{:S(2)}) %collective-permute-start.10) | collective-permute-done | bytes 262176 | tf_op jit(solution)/shard_map/ppermute | solution.py:132
  274.9 5.4 %copy.83 = f32[512,2048]{1,0:T(8,128)} copy(f32[512,2048]{0,1:T(8,128)} %get-tuple-element.52) | data formatting | bytes 8388608
  280.3 4.2 %add.345 = f32[512,2048]{1,0:T(8,128)S(1)} add(f32[512,2048]{1,0:T(8,128)} %copy.83, f32[512,2048]{1,0:T(8,128)} %collective-permute-done.13) | non-fusion elementwise | flops 1048576 | bytes 12582912 | tf_op jit(solution)/shard_map/add | solution.py:126
  284.5 2.0 copy-done.2
  286.5 1.8 constant_dynamic-slice_fusion.2
  288.3 1.4 collective-permute-start.16
  290.4 1.4 collective-permute-start.14
  293.3 3.2 fusion.16
  296.6 1.6 collective-permute-start.2
  298.2 6.3 %collective-permute-done.16 = f32[128,2048]{1,0:T(8,128)} collective-permute-done((f32[128,2048]{1,0:T(8,128)}, f32[128,2048]{1,0:T(8,128)}, u32[]{:S(2)}, u32[]{:S(2)}) %collective-permute-start.16) | collective-permute-done | bytes 1048608 | tf_op jit(solution)/shard_map/ppermute | solution.py:126
  304.5 11.1 %collective-permute-done.15 = f32[128,2048]{1,0:T(8,128)} collective-permute-done((f32[128,2048]{1,0:T(8,128)}, f32[128,2048]{1,0:T(8,128)}, u32[]{:S(2)}, u32[]{:S(2)}) %collective-permute-start.15) | collective-permute-done | bytes 1048608 | tf_op jit(solution)/shard_map/ppermute | solution.py:126
  315.6 2.4 add_add_fusion
  318.1 3.3 collective-permute-start.19
  322.7 2.1 collective-permute-start.17
  324.9 6.4 %collective-permute-done.19 = f32[32,2048]{1,0:T(8,128)S(1)} collective-permute-done((f32[32,2048]{1,0:T(8,128)S(1)}, f32[32,2048]{1,0:T(8,128)S(1)}, u32[]{:S(2)}, u32[]{:S(2)}) %collective-permute-start.19) | collective-permute-done | bytes 262176 | tf_op jit(solution)/shard_map/ppermute | solution.py:126
  331.4 3.2 collective-permute-done.18
  334.7 3.0 collective-permute-start.20
  338.9 2.4 collective-permute-done.20
  (235 shorter events, 45.1 us)
Async XLA Ops:
  7.2 91.5 %all-gather.3.cloned.1.call-start = ((), (), s32[]{:S(2)}) async-start(), calls=%async_computation | async-start | bytes 1064960 | tf_op jit(solution)/shard_map/all_gather | solution.py:212
  8.8 19.8 %copy-start.34 = (f32[1024]{0:T(1024)}, f32[1024]{0:T(1024)S(1)}, u32[]{:S(2)}) copy-start(f32[1024]{0:T(1024)S(1)} %get-tuple-element.43) | copy-start | bytes 12292
  24.3 38.3 %collective-permute-start = (bf16[512,1024]{1,0:T(8,128)(2,1)}, bf16[512,1024]{1,0:T(8,128)(2,1)}, u32[]{:S(2)}, u32[]{:S(2)}) collective-permute-start(bf16[512,1024]{1,0:T(8,128)(2,1)} %slice.204), channel_id=1, source_target_pairs={{0,2},{2,4},{4,6},{6,8},{8,10},{10,12},{12,14},{14,16},{16,18},{18... | collective-permute-start | bytes 3145736 | tf_op jit(solution)/shard_map/ppermute | solution.py:18
  29.2 7.4 %copy-start.1 = (bf16[1024,4,512]{2,1,0:T(4,128)(2,1)S(1)}, bf16[1024,4,512]{2,1,0:T(4,128)(2,1)}, u32[]{:S(2)}) copy-start(bf16[1024,4,512]{2,1,0:T(4,128)(2,1)} %param.30) | copy-start | bytes 12582916
  42.0 5.7 %copy-start.55 = (s32[64]{0:T(128)S(1)}, s32[64]{0:T(128)}, u32[]{:S(2)}) copy-start(s32[64]{0:T(128)} %constant.216.clone) | copy-start | bytes 772
  42.9 6.3 %copy-start.42 = (s32[64]{0:T(128)S(1)}, s32[64]{0:T(128)}, u32[]{:S(2)}) copy-start(s32[64]{0:T(128)} %param.32) | copy-start | bytes 772
  49.2 8.1 %copy-start.25 = (bf16[512,3,2,4,16]{0,4,3,2,1:T(8,128)(2,1)S(1)}, bf16[512,3,2,4,16]{0,4,3,2,1:T(8,128)(2,1)}, u32[]{:S(2)}) copy-start(bf16[512,3,2,4,16]{0,4,3,2,1:T(8,128)(2,1)} %slice.222) | copy-start | bytes 1179652
  49.2 8.1 %copy-start.33 = (bf16[512,1,2,4,16]{0,4,3,2,1:T(8,128)(2,1)S(1)}, bf16[512,1,2,4,16]{0,4,3,2,1:T(8,128)(2,1)}, u32[]{:S(2)}) copy-start(bf16[512,1,2,4,16]{0,4,3,2,1:T(8,128)(2,1)} %slice.221) | copy-start | bytes 393220
  58.6 42.5 %copy-start.38 = (pred[64]{0:T(512)(128)(4,1)}, pred[64]{0:T(512)(128)(4,1)S(1)}, u32[]{:S(2)}) copy-start(pred[64]{0:T(512)(128)(4,1)S(1)} %compare_and_fusion) | copy-start | bytes 196
  71.1 29.8 %copy-start.21 = (bf16[64,1024]{1,0:T(8,128)(2,1)S(1)}, bf16[64,1024]{1,0:T(8,128)(2,1)}, u32[]{:S(2)}) copy-start(bf16[64,1024]{1,0:T(8,128)(2,1)} %param.31) | copy-start | bytes 393220
  101.6 13.6 %copy-start.26 = (bf16[64,1024]{1,0:T(8,128)(2,1)}, bf16[64,1024]{1,0:T(8,128)(2,1)S(1)}, u32[]{:S(2)}) copy-start(bf16[64,1024]{1,0:T(8,128)(2,1)S(1)} %fusion.22) | copy-start | bytes 393220
  105.9 9.3 %copy-start.11 = (f32[8,512,64]{1,2,0:T(8,128)}, f32[8,512,64]{1,2,0:T(8,128)S(1)}, u32[]{:S(2)}) copy-start(f32[8,512,64]{1,2,0:T(8,128)S(1)} %get-tuple-element.79) | copy-start | bytes 3145732
  117.7 27.7 %copy-start.12 = (f32[8,512,64]{1,2,0:T(8,128)S(1)}, f32[8,512,64]{1,2,0:T(8,128)}, u32[]{:S(2)}) copy-start(f32[8,512,64]{1,2,0:T(8,128)} %copy-done.11) | copy-start | bytes 3145732
  117.7 27.7 %copy-start.14 = (bf16[512,512]{0,1:T(8,128)(2,1)S(1)}, bf16[512,512]{0,1:T(8,128)(2,1)}, u32[]{:S(2)}) copy-start(bf16[512,512]{0,1:T(8,128)(2,1)} %convolution_convert_fusion.1) | copy-start | bytes 1572868
  117.7 27.7 %copy-start.31 = (bf16[64,512]{0,1:T(8,128)(2,1)S(1)}, bf16[64,512]{0,1:T(8,128)(2,1)}, u32[]{:S(2)}) copy-start(bf16[64,512]{0,1:T(8,128)(2,1)} %copy.86) | copy-start | bytes 196612
  145.4 6.6 %slice-start = ((s8[8388608]{0:T(1024)(128)(4,1)}), s8[4194304]{0:T(1024)(128)(4,1)S(1)}, s32[]{:S(2)}) async-start(s8[8388608]{0:T(1024)(128)(4,1)} %bitcast.143), calls=%async_computation.1 | async-start | bytes 8388608
  152.0 13.1 %copy-start.4 = (f32[1024,8,64]{0,2,1:T(8,128)}, f32[1024,8,64]{0,2,1:T(8,128)S(1)}, u32[]{:S(2)}) copy-start(f32[1024,8,64]{0,2,1:T(8,128)S(1)} %convolution_bitcast_fusion) | copy-start | bytes 6291460
  169.9 5.7 %copy-start.10 = (f32[8,64,512]{2,1,0:T(8,128)S(1)}, f32[8,64,512]{2,1,0:T(8,128)}, u32[]{:S(2)}) copy-start(f32[8,64,512]{2,1,0:T(8,128)} %fusion.43) | copy-start | bytes 3145732
  169.9 5.7 %copy-start.32 = (bf16[64,512]{0,1:T(8,128)(2,1)S(1)}, bf16[64,512]{0,1:T(8,128)(2,1)}, u32[]{:S(2)}) copy-start(bf16[64,512]{0,1:T(8,128)(2,1)} %copy.86) | copy-start | bytes 196612
  172.3 14.1 %collective-permute-start.1 = (bf16[512,1024]{0,1:T(8,128)(2,1)S(1)}, bf16[512,1024]{0,1:T(8,128)(2,1)S(1)}, u32[]{:S(2)}, u32[]{:S(2)}) collective-permute-start(bf16[512,1024]{0,1:T(8,128)(2,1)S(1)} %pad_maximum_fusion.4), channel_id=1, source_target_pairs={{2,0},{4,2},{6,4},{8,6},{10,8},{12,10},{14,12},{16,14},{18,16},{20... | collective-permute-start | bytes 3145736 | tf_op jit(solution)/shard_map/ppermute | solution.py:18
  175.1 9.4 %copy-start.16 = (f32[8,64,64]{2,1,0:T(8,128)}, f32[8,64,64]{2,1,0:T(8,128)S(1)}, u32[]{:S(2)}) copy-start(f32[8,64,64]{2,1,0:T(8,128)S(1)} %fusion.42) | copy-start | bytes 393220
  175.6 8.9 %copy-start.18 = (f32[8,64,64]{2,1,0:T(8,128)}, f32[8,64,64]{2,1,0:T(8,128)S(1)}, u32[]{:S(2)}) copy-start(f32[8,64,64]{2,1,0:T(8,128)S(1)} %fusion.41) | copy-start | bytes 393220
  178.1 6.1 %copy-start.28 = (bf16[64,512]{0,1:T(8,128)(2,1)S(1)}, bf16[64,512]{0,1:T(8,128)(2,1)}, u32[]{:S(2)}) copy-start(bf16[64,512]{0,1:T(8,128)(2,1)} %copy.85) | copy-start | bytes 196612
  206.6 7.9 %copy-start.17 = (f32[8,64,64]{2,1,0:T(8,128)S(1)}, f32[8,64,64]{2,1,0:T(8,128)}, u32[]{:S(2)}) copy-start(f32[8,64,64]{2,1,0:T(8,128)} %copy-done.16) | copy-start | bytes 393220
  206.6 7.9 %copy-start.19 = (f32[8,64,64]{2,1,0:T(8,128)S(1)}, f32[8,64,64]{2,1,0:T(8,128)}, u32[]{:S(2)}) copy-start(f32[8,64,64]{2,1,0:T(8,128)} %copy-done.18) | copy-start | bytes 393220
  206.6 12.8 %copy-start.54 = (s32[64]{0:T(128)S(1)}, s32[64]{0:T(128)}, u32[]{:S(2)}) copy-start(s32[64]{0:T(128)} %constant.218.clone) | copy-start | bytes 772
  212.1 21.6 %copy-start.53 = (s32[64]{0:T(128)S(1)}, s32[64]{0:T(128)}, u32[]{:S(2)}) copy-start(s32[64]{0:T(128)} %constant.222.clone) | copy-start | bytes 772
  212.1 68.2 %collective-permute-start.13 = (f32[512,2048]{1,0:T(8,128)}, f32[512,2048]{1,0:T(8,128)}, u32[]{:S(2)}, u32[]{:S(2)}) collective-permute-start(f32[512,2048]{1,0:T(8,128)} %copy.84), channel_id=1, source_target_pairs={{0,2},{2,0},{4,6},{6,4},{8,10},{10,8},{12,14},{14,12},{16,18},{18,... | collective-permute-start | bytes 12582920 | tf_op jit(solution)/shard_map/ppermute | solution.py:126
  215.8 33.4 %copy-start.52 = (s32[64]{0:T(128)S(1)}, s32[64]{0:T(128)}, u32[]{:S(2)}) copy-start(s32[64]{0:T(128)} %constant.228.clone) | copy-start | bytes 772
  215.8 8.1 %collective-permute-start.5 = (f32[64,1024]{1,0:T(8,128)S(1)}, f32[64,1024]{1,0:T(8,128)S(1)}, u32[]{:S(2)}, u32[]{:S(2)}) collective-permute-start(f32[64,1024]{1,0:T(8,128)S(1)} %fusion.20), channel_id=1, source_target_pairs={{0,36},{2,110},{4,32},{6,106},{8,44},{10,102},{12,40},{14,98},{16,... | collective-permute-start | bytes 786440 | tf_op jit(solution)/shard_map/ppermute | solution.py:132
  216.1 9.8 %collective-permute-start.4 = (f32[64,1024]{1,0:T(8,128)S(1)}, f32[64,1024]{1,0:T(8,128)S(1)}, u32[]{:S(2)}, u32[]{:S(2)}) collective-permute-start(f32[64,1024]{1,0:T(8,128)S(1)} %fusion.20), channel_id=1, source_target_pairs={{0,4},{2,14},{4,0},{6,10},{8,12},{10,6},{12,8},{14,2},{16,20},{18,... | collective-permute-start | bytes 786440 | tf_op jit(solution)/shard_map/ppermute | solution.py:132
  219.0 7.0 %collective-permute-start.3 = (f32[64,1024]{1,0:T(8,128)S(1)}, f32[64,1024]{1,0:T(8,128)S(1)}, u32[]{:S(2)}, u32[]{:S(2)}) collective-permute-start(f32[64,1024]{1,0:T(8,128)S(1)} %fusion.20), channel_id=1, source_target_pairs={{0,32},{2,98},{4,36},{6,102},{8,40},{10,106},{12,44},{14,110},{16,... | collective-permute-start | bytes 786440 | tf_op jit(solution)/shard_map/ppermute | solution.py:132
  226.1 12.5 %collective-permute-start.8 = (f32[64,1024]{1,0:T(8,128)S(1)}, f32[64,1024]{1,0:T(8,128)S(1)}, u32[]{:S(2)}, u32[]{:S(2)}) collective-permute-start(f32[64,1024]{1,0:T(8,128)S(1)} %fusion.81), channel_id=1, source_target_pairs={{0,72},{2,74},{4,76},{6,78},{8,64},{10,66},{12,68},{14,70},{16,88}... | collective-permute-start | bytes 786440 | tf_op jit(solution)/shard_map/ppermute | solution.py:132
  232.8 12.7 %collective-permute-start.7 = (f32[64,1024]{1,0:T(8,128)S(1)}, f32[64,1024]{1,0:T(8,128)S(1)}, u32[]{:S(2)}, u32[]{:S(2)}) collective-permute-start(f32[64,1024]{1,0:T(8,128)S(1)} %fusion.81), channel_id=1, source_target_pairs={{0,8},{2,10},{4,12},{6,14},{8,0},{10,2},{12,4},{14,6},{16,24},{18,... | collective-permute-start | bytes 786440 | tf_op jit(solution)/shard_map/ppermute | solution.py:132
  232.8 12.7 %collective-permute-start.6 = (f32[64,1024]{1,0:T(8,128)S(1)}, f32[64,1024]{1,0:T(8,128)S(1)}, u32[]{:S(2)}, u32[]{:S(2)}) collective-permute-start(f32[64,1024]{1,0:T(8,128)S(1)} %fusion.81), channel_id=1, source_target_pairs={{0,64},{2,66},{4,68},{6,70},{8,72},{10,74},{12,76},{14,78},{16,80}... | collective-permute-start | bytes 786440 | tf_op jit(solution)/shard_map/ppermute | solution.py:132
  238.2 24.1 %copy-start.51 = (s32[64]{0:T(128)S(1)}, s32[64]{0:T(128)}, u32[]{:S(2)}) copy-start(s32[64]{0:T(128)} %constant.219.clone) | copy-start | bytes 772
  238.2 25.5 %copy-start.50 = (s32[64]{0:T(128)S(1)}, s32[64]{0:T(128)}, u32[]{:S(2)}) copy-start(s32[64]{0:T(128)} %constant.221.clone) | copy-start | bytes 772
  238.3 26.8 %copy-start.49 = (s32[64]{0:T(128)S(1)}, s32[64]{0:T(128)}, u32[]{:S(2)}) copy-start(s32[64]{0:T(128)} %constant.220.clone) | copy-start | bytes 772
  238.3 28.5 %copy-start.48 = (s32[64]{0:T(128)S(1)}, s32[64]{0:T(128)}, u32[]{:S(2)}) copy-start(s32[64]{0:T(128)} %constant.223.clone) | copy-start | bytes 772
  238.3 29.8 %copy-start.47 = (s32[64]{0:T(128)S(1)}, s32[64]{0:T(128)}, u32[]{:S(2)}) copy-start(s32[64]{0:T(128)} %constant.225.clone) | copy-start | bytes 772
  238.3 30.9 %copy-start.46 = (s32[64]{0:T(128)S(1)}, s32[64]{0:T(128)}, u32[]{:S(2)}) copy-start(s32[64]{0:T(128)} %constant.224.clone) | copy-start | bytes 772
  238.3 33.0 %copy-start.45 = (s32[64]{0:T(128)S(1)}, s32[64]{0:T(128)}, u32[]{:S(2)}) copy-start(s32[64]{0:T(128)} %constant.227.clone) | copy-start | bytes 772
  238.3 34.2 %copy-start.44 = (s32[64]{0:T(128)S(1)}, s32[64]{0:T(128)}, u32[]{:S(2)}) copy-start(s32[64]{0:T(128)} %constant.226.clone) | copy-start | bytes 772
  238.3 35.3 %copy-start.37 = (f32[512]{0:T(512)S(1)}, f32[512]{0:T(512)}, u32[]{:S(2)}) copy-start(f32[512]{0:T(512)} %copy-done.36) | copy-start | bytes 6148
  238.3 35.4 %copy-start.39 = (pred[64]{0:T(512)(128)(4,1)S(1)}, pred[64]{0:T(512)(128)(4,1)}, u32[]{:S(2)}) copy-start(pred[64]{0:T(512)(128)(4,1)} %copy-done.38) | copy-start | bytes 196
  238.3 35.4 %copy-start.41 = (f32[64]{0:T(128)S(1)}, f32[64]{0:T(128)}, u32[]{:S(2)}) copy-start(f32[64]{0:T(128)} %copy-done.40) | copy-start | bytes 772
  245.7 10.0 %collective-permute-start.11 = (f32[64,1024]{1,0:T(8,128)S(1)}, f32[64,1024]{1,0:T(8,128)S(1)}, u32[]{:S(2)}, u32[]{:S(2)}) collective-permute-start(f32[64,1024]{1,0:T(8,128)S(1)} %fusion.80), channel_id=1, source_target_pairs={{0,18},{2,16},{4,22},{6,20},{8,26},{10,24},{12,30},{14,28},{16,2},... | collective-permute-start | bytes 786440 | tf_op jit(solution)/shard_map/ppermute | solution.py:132
  247.0 14.5 %collective-permute-start.10 = (f32[64,1024]{1,0:T(8,128)S(1)}, f32[64,1024]{1,0:T(8,128)S(1)}, u32[]{:S(2)}, u32[]{:S(2)}) collective-permute-start(f32[64,1024]{1,0:T(8,128)S(1)} %fusion.80), channel_id=1, source_target_pairs={{0,16},{2,18},{4,20},{6,22},{8,24},{10,26},{12,28},{14,30},{16,0},... | collective-permute-start | bytes 786440 | tf_op jit(solution)/shard_map/ppermute | solution.py:132
  248.9 12.6 %collective-permute-start.9 = (f32[64,1024]{1,0:T(8,128)S(1)}, f32[64,1024]{1,0:T(8,128)S(1)}, u32[]{:S(2)}, u32[]{:S(2)}) collective-permute-start(f32[64,1024]{1,0:T(8,128)S(1)} %fusion.80), channel_id=1, source_target_pairs={{0,2},{2,0},{4,6},{6,4},{8,10},{10,8},{12,14},{14,12},{16,18},{18,... | collective-permute-start | bytes 786440 | tf_op jit(solution)/shard_map/ppermute | solution.py:132
  261.7 12.0 %collective-permute-start.12 = (f32[64,1024]{1,0:T(8,128)S(1)}, f32[64,1024]{1,0:T(8,128)S(1)}, u32[]{:S(2)}, u32[]{:S(2)}) collective-permute-start(f32[64,1024]{1,0:T(8,128)S(1)} %add_bitcast_fusion), channel_id=1, source_target_pairs={{0,1},{1,0},{2,3},{3,2},{4,5},{5,4},{6,7},{7,6},{8,9},{9,8},{10,11... | collective-permute-start | bytes 786440 | tf_op jit(solution)/shard_map/ppermute | solution.py:135
  286.5 5.3 %copy-start.30 = (f32[64,1024]{1,0:T(8,128)S(1)}, f32[64,1024]{1,0:T(8,128)}, u32[]{:S(2)}) copy-start(f32[64,1024]{1,0:T(8,128)} %subtract_multiply_fusion) | copy-start | bytes 786436
  286.5 5.3 %copy-start.43 = (s32[64]{0:T(128)S(1)}, s32[64]{0:T(128)}, u32[]{:S(2)}) copy-start(s32[64]{0:T(128)} %param.32) | copy-start | bytes 772
  286.5 5.5 %copy-start.35 = (f32[1024]{0:T(1024)S(1)}, f32[1024]{0:T(1024)}, u32[]{:S(2)}) copy-start(f32[1024]{0:T(1024)} %copy-done.34) | copy-start | bytes 12292
  286.5 6.8 %copy-start.13 = (bf16[1024,3,512]{0,2,1:T(8,128)(2,1)S(1)}, bf16[1024,3,512]{0,2,1:T(8,128)(2,1)}, u32[]{:S(2)}) copy-start(bf16[1024,3,512]{0,2,1:T(8,128)(2,1)} %copy.79) | copy-start | bytes 9437188
  288.3 16.1 %collective-permute-start.16 = (f32[128,2048]{1,0:T(8,128)}, f32[128,2048]{1,0:T(8,128)}, u32[]{:S(2)}, u32[]{:S(2)}) collective-permute-start(f32[128,2048]{1,0:T(8,128)} %get-tuple-element.54), channel_id=1, source_target_pairs={{0,36},{2,110},{4,32},{6,106},{8,44},{10,102},{12,40},{14,98},{16,... | collective-permute-start | bytes 3145736 | tf_op jit(solution)/shard_map/ppermute | solution.py:126
  289.7 25.9 %collective-permute-start.15 = (f32[128,2048]{1,0:T(8,128)}, f32[128,2048]{1,0:T(8,128)}, u32[]{:S(2)}, u32[]{:S(2)}) collective-permute-start(f32[128,2048]{1,0:T(8,128)} %get-tuple-element.55), channel_id=1, source_target_pairs={{0,4},{2,14},{4,0},{6,10},{8,12},{10,6},{12,8},{14,2},{16,20},{18,... | collective-permute-start | bytes 3145736 | tf_op jit(solution)/shard_map/ppermute | solution.py:126
  290.4 25.2 %collective-permute-start.14 = (f32[128,2048]{1,0:T(8,128)}, f32[128,2048]{1,0:T(8,128)}, u32[]{:S(2)}, u32[]{:S(2)}) collective-permute-start(f32[128,2048]{1,0:T(8,128)} %get-tuple-element.53), channel_id=1, source_target_pairs={{0,32},{2,98},{4,36},{6,102},{8,40},{10,106},{12,44},{14,110},{16,... | collective-permute-start | bytes 3145736 | tf_op jit(solution)/shard_map/ppermute | solution.py:126
  296.5 28.2 %copy-start.5 = (f32[512,1024]{1,0:T(8,128)S(1)}, f32[512,1024]{1,0:T(8,128)}, u32[]{:S(2)}) copy-start(f32[512,1024]{1,0:T(8,128)} %get-tuple-element.60) | copy-start | bytes 6291460
  296.6 28.1 %collective-permute-start.2 = (bf16[256,1024]{1,0:T(8,128)(2,1)S(1)}, bf16[256,1024]{1,0:T(8,128)(2,1)S(1)}, u32[]{:S(2)}, u32[]{:S(2)}) collective-permute-start(bf16[256,1024]{1,0:T(8,128)(2,1)S(1)} %dynamic-slice_convert_fusion), channel_id=1, source_target_pairs={{0,1},{1,0},{2,3},{3,2},{4,5},{5,4},{6,7},{7,6},{8,9},{9,8},{10,11... | collective-permute-start | bytes 1572872 | tf_op jit(solution)/shard_map/ppermute | solution.py:291
  318.0 19.7 %copy-start.15 = (bf16[512,1024]{1,0:T(8,128)(2,1)S(1)}, bf16[512,1024]{1,0:T(8,128)(2,1)}, u32[]{:S(2)}) copy-start(bf16[512,1024]{1,0:T(8,128)(2,1)} %param.29) | copy-start | bytes 3145732
  318.1 13.3 %collective-permute-start.19 = (f32[32,2048]{1,0:T(8,128)S(1)}, f32[32,2048]{1,0:T(8,128)S(1)}, u32[]{:S(2)}, u32[]{:S(2)}) collective-permute-start(f32[32,2048]{1,0:T(8,128)S(1)} %get-tuple-element.62), channel_id=1, source_target_pairs={{0,72},{2,74},{4,76},{6,78},{8,64},{10,66},{12,68},{14,70},{16,88}... | collective-permute-start | bytes 786440 | tf_op jit(solution)/shard_map/ppermute | solution.py:126
  321.5 13.1 %collective-permute-start.18 = (f32[32,2048]{1,0:T(8,128)S(1)}, f32[32,2048]{1,0:T(8,128)S(1)}, u32[]{:S(2)}, u32[]{:S(2)}) collective-permute-start(f32[32,2048]{1,0:T(8,128)S(1)} %get-tuple-element.63), channel_id=1, source_target_pairs={{0,8},{2,10},{4,12},{6,14},{8,0},{10,2},{12,4},{14,6},{16,24},{18,... | collective-permute-start | bytes 786440 | tf_op jit(solution)/shard_map/ppermute | solution.py:126
  322.7 11.9 %collective-permute-start.17 = (f32[32,2048]{1,0:T(8,128)S(1)}, f32[32,2048]{1,0:T(8,128)S(1)}, u32[]{:S(2)}, u32[]{:S(2)}) collective-permute-start(f32[32,2048]{1,0:T(8,128)S(1)} %get-tuple-element.61), channel_id=1, source_target_pairs={{0,64},{2,66},{4,68},{6,70},{8,72},{10,74},{12,76},{14,78},{16,80}... | collective-permute-start | bytes 786440 | tf_op jit(solution)/shard_map/ppermute | solution.py:126
  334.7 6.6 %collective-permute-start.20 = (f32[16,2048]{1,0:T(8,128)S(1)}, f32[16,2048]{1,0:T(8,128)S(1)}, u32[]{:S(2)}, u32[]{:S(2)}) collective-permute-start(f32[16,2048]{1,0:T(8,128)S(1)} %constant_dynamic-slice_fusion.8), channel_id=1, source_target_pairs={{0,16},{2,18},{4,20},{6,22},{8,24},{10,26},{12,28},{14,30},{16,0},... | collective-permute-start | bytes 393224 | tf_op jit(solution)/shard_map/ppermute | solution.py:126
  (19 other events, 57.0 us)
Sparse Core Ops, SparseCore 0:
  29.3 69.2 all-gather.2
